TPU v7x, 128 devices: a whole 4x4x4 slice. The times are simulated.
128 devices in a mesh: sample: 8 (over x, y_hi), landmark: 16 (over z, y_lo, core).
Axes of the slice: x: 4, y: 4 (y_hi: 2, y_lo: 2; y = y_hi * 2 + y_lo), z: 4, core: 2. Of those that a mesh axis runs over, the one named last changes fastest.
Arguments:
- summaries: bfloat16 [16384, 1024], P('sample', 'landmark'), may hold values from -12 to 12
- row_level: int32 [16384], P('sample'), may hold values from 0 to 3
- pool: bfloat16 [32768, 1024], P('landmark'), may hold values from -6 to 6
- pool_level: int32 [32768], P('landmark'), may hold values from 0 to 3
- landmark_index: int32 [16384], P('landmark'), may hold values from 0 to 2047, as said below
- level_scale: float32 [4], replicated, may hold values from 1.2 to 2.4
- targets: bfloat16 [16384, 256], P('sample'), may hold values from -6 to 6
Outputs:
- weights: float32 [16384, 256], P('landmark')
- residual: float32 [16384, 256], P('landmark')
Inputs may be any that keep to these rules, and one draw needn't show every extreme that they name: Landmark j is pool row (j // 1024) * 2048 + landmark_index[j], a row of the pool block of its own landmark group; indices may repeat.
All inputs are finite; a program needn't handle non-finite values.
Results may differ from a plain program's by a relative error of at most 0.012.
Values may be sent and summed in bfloat16 or wider, within the bound.
No kernel may reach another device: no remote copies, remote signals or barrier semaphores. Data moves between devices by JAX's collectives and lax.ppermute only.
A program may use at most 64 MiB of HBM per device.

v0:
```python
import math
import jax
import jax.numpy as jnp
from jax import lax
from jax.sharding import PartitionSpec as P

ITERS = 2
GROUPS = 1


def REDUCE(x, extra, axis, bits, gather_dtype, wire_dtype=jnp.bfloat16):
    return exchange_sum(x, extra, axis, gather_dtype, wire_dtype)


ridge = 0.5


def level_values(level_ids, level_table):
    onehot = level_ids[:, None] == jnp.arange(level_table.shape[0], dtype=jnp.int32)[None, :]
    return jnp.sum(
        jnp.where(onehot, level_table[None, :], jnp.zeros_like(level_table)[None, :]), axis=1
    )


def raw_block(summary_rows, row_factor, anchors, anchor_factor):
    scores = jnp.dot(summary_rows, anchors.T, preferred_element_type=jnp.float32)
    return jnp.exp(scores * row_factor[:, None] * anchor_factor[None, :])


def partner_bits(size, order):
    bits = [b for b in order if b < size]
    assert sorted(bits) == [1 << i for i in range(size.bit_length() - 1)]
    return bits


def butterfly_sum(x, axis, bits):
    size = lax.axis_size(axis)
    for k in bits:
        perm = [(i, i ^ k) for i in range(size)]
        x = x + lax.ppermute(x, axis, perm)
    return x


def pack_rows(extra, columns, wire_dtype):
    rows = extra.reshape(-1, columns)
    if wire_dtype == jnp.float32:
        parts = [rows]
    else:
        parts = []
        rest = rows
        for _ in range(3):
            term = lax.reduce_precision(rest, exponent_bits=8, mantissa_bits=7)
            parts.append(term)
            rest = rest - term
    return jnp.concatenate(parts, axis=0).astype(wire_dtype)


def unpack_rows(packed, count, wire_dtype):
    terms = 1 if wire_dtype == jnp.float32 else 3
    packed = packed.astype(jnp.float32).reshape(terms, count, -1)
    total = packed[0]
    for t in range(1, terms):
        total = total + packed[t]
    return total.reshape(-1)


def halving_sum(x, extra, axis, bits, gather_dtype, wire_dtype=jnp.bfloat16):
    size = lax.axis_size(axis)
    index = lax.axis_index(axis)
    columns = x.shape[1]
    for k in bits:
        perm = [(i, i ^ k) for i in range(size)]
        half = x.shape[0] // 2
        mine = index // k % 2
        keep = lax.dynamic_slice_in_dim(x, mine * half, half, axis=0)
        send = lax.dynamic_slice_in_dim(x, (1 - mine) * half, half, axis=0).astype(wire_dtype)
        if extra is not None:
            send = jnp.concatenate([send, pack_rows(extra, columns, wire_dtype)], axis=0)
        got = lax.ppermute(send, axis, perm)
        x = keep + got[:half].astype(jnp.float32)
        if extra is not None:
            extra = extra + unpack_rows(got[half:], extra.shape[0] // columns, wire_dtype)
    x = x.astype(gather_dtype)
    for k in reversed(bits):
        perm = [(i, i ^ k) for i in range(size)]
        part = x.shape[0]
        mine = index // k % 2
        got = lax.ppermute(x, axis, perm)
        whole = jnp.zeros((2 * part,) + x.shape[1:], x.dtype)
        whole = lax.dynamic_update_slice_in_dim(whole, x, mine * part, axis=0)
        x = lax.dynamic_update_slice_in_dim(whole, got, (1 - mine) * part, axis=0)
    return (x, extra)


def exchange_scatter(x, extra, axis, wire_dtype):
    size = lax.axis_size(axis)
    rows, columns = x.shape
    chunks = x.reshape(size, rows // size, columns).astype(wire_dtype)
    if extra is not None:
        packed = pack_rows(extra, columns, wire_dtype)
        chunks = jnp.concatenate(
            [chunks, jnp.broadcast_to(packed[None], (size,) + packed.shape)], axis=1
        )
    got = lax.all_to_all(chunks, axis, 0, 0, tiled=False)
    total = jnp.sum(got.astype(jnp.float32), axis=0)
    part = total[: rows // size]
    if extra is not None:
        extra = unpack_rows(total[rows // size :], extra.shape[0] // columns, wire_dtype)
    return (part, extra)


def exchange_gather(part, axis):
    size = lax.axis_size(axis)
    whole = lax.all_to_all(
        jnp.broadcast_to(part[None], (size,) + part.shape), axis, 0, 0, tiled=False
    )
    return whole.reshape((size * part.shape[0],) + part.shape[1:])


def exchange_sum(x, extra, axis, gather_dtype, wire_dtype=jnp.bfloat16):
    part, extra = exchange_scatter(x, extra, axis, wire_dtype)
    return (exchange_gather(part.astype(gather_dtype), axis), extra)


def native_scatter(x, extra, axis):
    size = lax.axis_size(axis)
    rows, columns = x.shape
    chunks = x.reshape(size, rows // size, columns)
    packed = extra.reshape(-1, columns)
    chunks = jnp.concatenate(
        [chunks, jnp.broadcast_to(packed[None], (size,) + packed.shape)], axis=1
    )
    total = lax.psum_scatter(chunks, axis, scatter_dimension=0, tiled=False)
    return (total[: rows // size], total[rows // size :].reshape(-1))


def native_gather(part, axis):
    return lax.all_gather(part, axis, axis=0, tiled=True)


def conjugate_gradients(kernel, targets, n_rows, sample_bits, landmark_bits):
    rhs_part = jnp.dot(kernel.T, targets, preferred_element_type=jnp.float32)
    rhs_total, _ = exchange_sum(rhs_part, None, "sample", jnp.float32, jnp.float32)
    rhs = rhs_total / math.sqrt(n_rows)
    column_count = rhs.shape[1]
    weights = jnp.zeros_like(rhs)
    residual = rhs
    direction = rhs
    for iteration in range(ITERS):
        if iteration == 0:
            row_part = jnp.dot(
                kernel, direction.astype(jnp.bfloat16), preferred_element_type=jnp.float32
            )
            sums = jnp.concatenate(
                [jnp.sum(direction * direction, axis=0), jnp.sum(residual * residual, axis=0)]
            )
            row_chunk, landmark_sums = native_scatter(row_part, sums, "landmark")
            direction_square = landmark_sums[:column_count]
            norm_now = landmark_sums[column_count:]
        else:
            row_part = jnp.dot(
                kernel, residual.astype(jnp.bfloat16), preferred_element_type=jnp.float32
            )
            sums = jnp.concatenate(
                [jnp.sum(residual * residual, axis=0), jnp.sum(residual * direction, axis=0)]
            )
            residual_chunk, landmark_sums = native_scatter(row_part, sums, "landmark")
            norm_next = landmark_sums[:column_count]
            cross = landmark_sums[column_count:]
            beta = norm_next / norm_now
            row_chunk = residual_chunk + beta * row_chunk
            direction = residual + beta * direction
            direction_square = norm_next + 2.0 * beta * cross + beta * beta * direction_square
            norm_now = norm_next
        row_half = native_gather(row_chunk.astype(jnp.bfloat16), "landmark")
        row_square = jnp.sum(jnp.square(row_half.astype(jnp.float32)), axis=0)
        column_part = jnp.dot(kernel.T, row_half, preferred_element_type=jnp.float32)
        column_total, row_square_total = exchange_sum(
            column_part, row_square, "sample", jnp.float32, jnp.float32
        )
        image = column_total / n_rows + ridge * direction
        curvature = row_square_total / n_rows + ridge * direction_square
        step_size = norm_now / curvature
        weights = weights + step_size * direction
        residual = residual - step_size * image
    return (weights, residual)


def on_device(summaries, row_level, pool, pool_level, landmark_index, level_scale, targets):
    sample_bits = partner_bits(lax.axis_size("sample"), (2, 1, 4, 8, 16, 32, 64))
    landmark_bits = partner_bits(lax.axis_size("landmark"), (1, 2, 4, 8, 16, 32, 64))
    row_count = summaries.shape[0]
    n_rows = row_count * lax.axis_size("sample")
    gathered = lax.all_gather(summaries, "landmark", axis=1, tiled=True)
    feature_count = gathered.shape[1]
    anchors = jnp.take(pool, landmark_index, axis=0)
    anchor_level = jnp.take(pool_level, landmark_index, axis=0)
    row_factor = 1.0 / math.sqrt(feature_count) / level_values(row_level, level_scale)
    anchor_factor = 1.0 / level_values(anchor_level, level_scale)
    raw = raw_block(gathered, row_factor, anchors, anchor_factor)
    column_mean = butterfly_sum(jnp.sum(raw, axis=0), "sample", sample_bits) / n_rows
    kernel = (raw - column_mean[None, :]).astype(jnp.bfloat16)
    column_count = targets.shape[1]
    group_width = column_count // GROUPS
    results = [
        conjugate_gradients(
            kernel,
            targets[:, g * group_width : (g + 1) * group_width],
            n_rows,
            sample_bits,
            landmark_bits,
        )
        for g in range(GROUPS)
    ]
    weights = jnp.concatenate([r[0] for r in results], axis=1)
    residual = jnp.concatenate([r[1] for r in results], axis=1)
    return (weights, residual)


def solution(mesh):
    return jax.shard_map(
        on_device,
        mesh=mesh,
        in_specs=(
            P("sample", "landmark"),
            P("sample"),
            P("landmark", None),
            P("landmark"),
            P("landmark"),
            P(),
            P("sample", None),
        ),
        out_specs=(P("landmark", None), P("landmark", None)),
        check_vma=False,
    )
```

profile of v0, /device:TPU:0, one launch (start us, length us, event | category | flops | bytes accessed | tf_op | source)
XLA Modules:
  0.0 430.9 jit_solution(6700054975939726392)
XLA Ops:
  8.6 5.7 %gather_fusion.1 = s32[1024]{0:T(1024)S(1)} fusion(s32[2048]{0:T(1024)} %param.10, s32[1024]{0:T(1024)S(1)} %fusion.14), kind=kCustom, calls=%fused_computation.1 | custom fusion | bytes 12288 | tf_op jit(solution)/shard_map/jit(_take)/gather | solution.py:197
  14.4 8.8 %gather_fusion = bf16[1024,1024]{1,0:T(8,128)(2,1)} fusion(bf16[2048,1024]{1,0:T(8,128)(2,1)} %param.9, s32[1024]{0:T(1024)S(1)} %fusion.14), kind=kCustom, calls=%fused_computation | custom fusion | bytes 4198400 | tf_op jit(solution)/shard_map/jit(_take)/gather | solution.py:196
  23.4 26.2 %all-gather.4.cloned.1.call-done = bf16[2048,1024]{0,1:T(8,128)(2,1)} async-done(((bf16[2048,64]{0,1:T(8,128)(2,1)}), bf16[2048,1024]{0,1:T(8,128)(2,1)}) %all-gather.4.cloned.1.call-update) | async-done | bytes 4194320 | tf_op jit(solution)/shard_map/all_gather | solution.py:194
  49.6 7.9 %fusion = (f32[1024]{0:T(1024)S(1)}, f32[1024,2048]{1,0:T(8,128)S(1)}) fusion(f32[1024]{0:T(1024)S(1)} %broadcast_divide_fusion.1, f32[2048]{0:T(1024)S(1)} %broadcast_divide_fusion, bf16[2048,1024]{0,1:T(8,128)(2,1)} %all-gather.4.cloned.1.call-done, bf16[1024,1024]{1,0:T(8,128)(2,1)} %gather_fusion, pred[1024]{0:T(1024)(128)(4,1)S(1)} %get-tuple-element.5), kind=kOutput, calls=%fused_computation.4 | convolution fusion | flops 4302306304 | bytes 14697472 | tf_op jit(solution)/shard_map/dot_general | solution.py:26
  75.2 20.1 %all_to_all.30 = f32[8,128,256]{2,1,0:T(8,128)S(1)} all-to-all(f32[8,128,256]{2,1,0:T(8,128)S(1)} %bitcast.108), channel_id=1, replica_groups=mesh['sample'=8,'landmark'=16] {'sample'}, dimensions={0} | all-to-all | bytes 2097152 | tf_op jit(solution)/shard_map/all_to_all | solution.py:104
  96.4 3.6 all-to-all-start.1
  100.2 5.6 %fusion.40 = bf16[2048,1024]{0,1:T(8,128)(2,1)} fusion(f32[1024]{0:T(1024)S(1)} %add_multiply_fusion, f32[1024]{0:T(1024)S(1)} %broadcast_divide_fusion.1, f32[1024,2048]{1,0:T(8,128)} %copy-done.1, f32[2048]{0:T(1024)S(1)} %broadcast_divide_fusion), kind=kLoop, calls=%fused_computation.74 | loop fusion | flops 8388608 | bytes 12599296 | tf_op jit(solution)/shard_map/sub | solution.py:202
  105.9 6.4 %copy.15 = bf16[2048,1024]{1,0:T(8,128)(2,1)} copy(bf16[2048,1024]{0,1:T(8,128)(2,1)} %fusion.40) | data formatting | bytes 8388608 | tf_op jit(solution)/shard_map/dot_general | solution.py:151
  112.5 3.5 fusion.25
  117.6 66.2 %reduce-scatter.3.cloned.1.call-done = f32[1,130,256]{2,1,0:T(8,128)} async-done(((f32[16,130,256]{2,1,0:T(8,128)}), f32[1,130,256]{2,1,0:T(8,128)}) %reduce-scatter.3.cloned.1.call-update) | async-done | bytes 133136 | tf_op jit(solution)/shard_map/reduce_scatter | solution.py:133
  185.4 31.5 %all-gather.6.cloned.1.call-done = bf16[2048,256]{1,0:T(8,128)(2,1)} async-done(((bf16[128,256]{1,0:T(8,128)(2,1)}), bf16[2048,256]{1,0:T(8,128)(2,1)}) %all-gather.6.cloned.1.call-update) | async-done | bytes 1048592 | tf_op jit(solution)/shard_map/all_gather | solution.py:138
  218.5 3.7 fusion.26
  222.3 24.5 %all_to_all.31 = f32[8,129,256]{2,1,0:T(8,128)S(1)} all-to-all(f32[8,129,256]{2,1,0:T(8,128)S(1)} %pad_maximum_fusion.2), channel_id=1, replica_groups=mesh['sample'=8,'landmark'=16] {'sample'}, dimensions={0} | all-to-all | bytes 2113536 | tf_op jit(solution)/shard_map/all_to_all | solution.py:104
  248.0 3.6 all-to-all-start.3
  251.7 14.9 %all-to-all-done.3 = f32[8,128,256]{2,1,0:T(8,128)S(1)} async-done(((f32[8,128,256]{2,1,0:T(8,128)}), f32[8,128,256]{2,1,0:T(8,128)S(1)}, u32[]{:S(2)}, u32[]{:S(2)}) %all-to-all-start.3) | async-done | bytes 1048608 | tf_op jit(solution)/shard_map/all_to_all | solution.py:114
  267.9 4.8 %fusion.27 = f32[16,128,256]{2,1,0:T(8,128)} fusion(bf16[16,128,1024]{2,1,0:T(8,128)(2,1)} %bitcast.105, bf16[1024,256,1]{1,0,2:T(8,128)(2,1)S(1)} %bitcast.110), kind=kOutput, calls=%fused_computation.72 | convolution fusion | flops 1073741824 | bytes 6815744 | tf_op jit(solution)/shard_map/dot_general | solution.py:161
  272.8 3.2 pad_maximum_fusion.1
  276.0 63.2 %reduce-scatter.5.cloned.1.call-done = f32[1,130,256]{2,1,0:T(8,128)} async-done(((f32[16,130,256]{2,1,0:T(8,128)}), f32[1,130,256]{2,1,0:T(8,128)}) %reduce-scatter.5.cloned.1.call-update) | async-done | bytes 133136 | tf_op jit(solution)/shard_map/reduce_scatter | solution.py:133
  341.6 31.0 %all-gather.8.cloned.1.call-done = bf16[2048,256]{1,0:T(8,128)(2,1)} async-done(((bf16[128,256]{1,0:T(8,128)(2,1)}), bf16[2048,256]{1,0:T(8,128)(2,1)}) %all-gather.8.cloned.1.call-update) | async-done | bytes 1048592 | tf_op jit(solution)/shard_map/all_gather | solution.py:138
  372.5 3.8 fusion.28
  376.8 24.5 %all_to_all.32 = f32[8,129,256]{2,1,0:T(8,128)S(1)} all-to-all(f32[8,129,256]{2,1,0:T(8,128)S(1)} %pad_maximum_fusion.3), channel_id=1, replica_groups=mesh['sample'=8,'landmark'=16] {'sample'}, dimensions={0} | all-to-all | bytes 2113536 | tf_op jit(solution)/shard_map/all_to_all | solution.py:104
  402.5 3.6 all-to-all-start.5
  406.9 14.2 %all-to-all-done.5 = f32[8,128,256]{2,1,0:T(8,128)S(1)} async-done(((f32[8,128,256]{2,1,0:T(8,128)}), f32[8,128,256]{2,1,0:T(8,128)S(1)}, u32[]{:S(2)}, u32[]{:S(2)}) %all-to-all-start.5) | async-done | bytes 1048608 | tf_op jit(solution)/shard_map/all_to_all | solution.py:114
  421.1 3.2 fusion.5
  (75 shorter events, 33.0 us)
Async XLA Ops:
  7.2 66.1 %copy-start = (bf16[2048,256]{1,0:T(8,128)(2,1)S(1)}, bf16[2048,256]{1,0:T(8,128)(2,1)}, u32[]{:S(2)}) copy-start(bf16[2048,256]{1,0:T(8,128)(2,1)} %param.13) | copy-start | bytes 3145732
  7.2 42.4 %all-gather.4.cloned.1.call-start = ((), (), s32[]{:S(2)}) async-start(), calls=%async_computation.8 | async-start | bytes 4456448 | tf_op jit(solution)/shard_map/all_gather | solution.py:194
  14.3 8.8 %copy-start.5 = (s32[1024]{0:T(1024)S(1)}, s32[1024]{0:T(1024)}, u32[]{:S(2)}) copy-start(s32[1024]{0:T(1024)} %param.11) | copy-start | bytes 12292
  14.4 8.8 %copy-start.7 = (f32[4]{0:T(128)S(1)}, f32[4]{0:T(128)}, u32[]{:S(2)}) copy-start(f32[4]{0:T(128)} %param.12) | copy-start | bytes 52
  14.4 8.9 %copy-start.6 = (s32[2048]{0:T(1024)S(1)}, s32[2048]{0:T(1024)}, u32[]{:S(2)}) copy-start(s32[2048]{0:T(1024)} %param.8) | copy-start | bytes 24580
  57.5 15.8 %copy-start.1 = (f32[1024,2048]{1,0:T(8,128)}, f32[1024,2048]{1,0:T(8,128)S(1)}, u32[]{:S(2)}) copy-start(f32[1024,2048]{1,0:T(8,128)S(1)} %get-tuple-element.13) | copy-start | bytes 25165828
  57.5 3.7 collective-permute-start
  61.2 5.1 %collective-permute-start.1 = (f32[1024]{0:T(1024)S(1)}, f32[1024]{0:T(1024)S(1)}, u32[]{:S(2)}, u32[]{:S(2)}) collective-permute-start(f32[1024]{0:T(1024)S(1)} %add.75), channel_id=1, source_target_pairs={{0,16},{16,0},{32,48},{48,32},{64,80},{80,64},{96,112},{112,96},{1... | collective-permute-start | bytes 12296 | tf_op jit(solution)/shard_map/ppermute | solution.py:40
  66.3 5.1 %collective-permute-start.2 = (f32[1024]{0:T(1024)S(1)}, f32[1024]{0:T(1024)S(1)}, u32[]{:S(2)}, u32[]{:S(2)}) collective-permute-start(f32[1024]{0:T(1024)S(1)} %add.76), channel_id=1, source_target_pairs={{0,64},{16,80},{32,96},{48,112},{64,0},{80,16},{96,32},{112,48},{1... | collective-permute-start | bytes 12296 | tf_op jit(solution)/shard_map/ppermute | solution.py:40
  73.2 2.0 copy-start.2
  96.4 15.8 %all-to-all-start.1 = ((f32[8,128,256]{2,1,0:T(8,128)}), f32[8,128,256]{2,1,0:T(8,128)S(1)}, u32[]{:S(2)}, u32[]{:S(2)}) async-start(f32[8,128,256]{2,1,0:T(8,128)} %broadcast_in_dim.115), calls=%async_computation.1 | async-start | bytes 2097152 | tf_op jit(solution)/shard_map/all_to_all | solution.py:114
  100.0 83.9 %reduce-scatter.3.cloned.1.call-start = ((), (), s32[]{:S(2)}) async-start(), calls=%async_computation.9 | async-start | bytes 2367488 | tf_op jit(solution)/shard_map/reduce_scatter | solution.py:133
  117.6 99.4 %all-gather.6.cloned.1.call-start = ((), (), s32[]{:S(2)}) async-start(), calls=%async_computation.10 | async-start | bytes 1114112 | tf_op jit(solution)/shard_map/all_gather | solution.py:138
  222.2 29.4 %copy-start.4 = (f32[1,130,256]{2,1,0:T(8,128)S(1)}, f32[1,130,256]{2,1,0:T(8,128)}, u32[]{:S(2)}) copy-start(f32[1,130,256]{2,1,0:T(8,128)} %reduce-scatter.3.cloned.1.call-done) | copy-start | bytes 399364
  248.0 18.6 %all-to-all-start.3 = ((f32[8,128,256]{2,1,0:T(8,128)}), f32[8,128,256]{2,1,0:T(8,128)S(1)}, u32[]{:S(2)}, u32[]{:S(2)}) async-start(f32[8,128,256]{2,1,0:T(8,128)} %broadcast_in_dim.119), calls=%async_computation.4 | async-start | bytes 2097152 | tf_op jit(solution)/shard_map/all_to_all | solution.py:114
  251.6 87.7 %reduce-scatter.5.cloned.1.call-start = ((), (), s32[]{:S(2)}) async-start(), calls=%async_computation.11 | async-start | bytes 2367488 | tf_op jit(solution)/shard_map/reduce_scatter | solution.py:133
  276.0 96.5 %all-gather.8.cloned.1.call-start = ((), (), s32[]{:S(2)}) async-start(), calls=%async_computation.12 | async-start | bytes 1114112 | tf_op jit(solution)/shard_map/all_gather | solution.py:138
  372.5 3.8 copy-start.3
  402.5 18.6 %all-to-all-start.5 = ((f32[8,128,256]{2,1,0:T(8,128)}), f32[8,128,256]{2,1,0:T(8,128)S(1)}, u32[]{:S(2)}, u32[]{:S(2)}) async-start(f32[8,128,256]{2,1,0:T(8,128)} %broadcast_in_dim.123), calls=%async_computation.7 | async-start | bytes 2097152 | tf_op jit(solution)/shard_map/all_to_all | solution.py:114
Sparse Core Ops, SparseCore 0:
  9.7 39.8 all-gather.3
  117.7 66.1 reduce-scatter.2
  186.1 30.7 all-gather.5
  276.1 63.1 reduce-scatter.4
  341.7 30.8 all-gather.7
where the time goes:
time: 432 us; the launch traced here: 431 us
  waiting for transfers between devices  255 us (59%)
  blocking collectives  69.1 us (16%)
  local copies, waits for them, and re-layouts  26.5 us (6%)
  matrix products  24.9 us (6%)
  other arithmetic  23.3 us (5%)
  starting transfers between devices  18.4 us (4%)
  between operations  14.1 us (3%)
    reduce_scatter x2, waiting for transfers between devices, native_scatter(): total = lax.psum_scatter(chunks, axis, scatter_dimension=0, tiled=False)  129 us
    all_to_all x3, blocking collectives, exchange_scatter(): got = lax.all_to_all(chunks, axis, 0, 0, tiled=False)  69.1 us
    all_gather x2, waiting for transfers between devices, native_gather(): return lax.all_gather(part, axis, axis=0, tiled=True)  62.5 us
    all_to_all x3, waiting for transfers between devices, exchange_gather(): lax.all_to_all(jnp.broadcast_to(part[None], (size,) + part.shape), axis,...  29.1 us
    all_gather x1, waiting for transfers between devices, on_device(): gathered = lax.all_gather(summaries, 'landmark', axis=1, tiled=True)  26.2 us
    all_to_all x3, starting transfers between devices, exchange_gather(): lax.all_to_all(jnp.broadcast_to(part[None], (size,) + part.shape), axis,...  10.7 us
    gather x1, local copies, waits for them, and re-layouts, on_device(): anchors = jnp.take(pool, landmark_index, axis=0)  8.79 us
  transfers between devices with their start and end apart: 11, of which 10 were waited for; matrix products, arithmetic and copies ran while one was open for 7% of the time, Pallas kernels for 0%

commit v1 on v0

--- a/solution.py
+++ b/solution.py
@@ -135,7 +135,9 @@
 
 
 def native_gather(part, axis):
-    return lax.all_gather(part, axis, axis=0, tiled=True)
+    return jnp.concatenate(
+        lax.all_to_all(jnp.stack([part] * lax.axis_size(axis)), axis, 0, 0), axis=0
+    )
 
 
 def conjugate_gradients(kernel, targets, n_rows, sample_bits, landmark_bits):

time: 432 us -> 401 us (0.928)
  waiting for transfers between devices: 255 us -> 191 us
  blocking collectives: 69.1 us -> 105 us
    all_gather x2 -> x0, waiting for transfers between devices: 62.5 us -> none  [native_gather(): return lax.all_gather(part, axis, axis=0, tiled=True)]
    all_to_all x0 -> x2, blocking collectives: none -> 38.1 us  [native_gather(): lax.all_to_all(jnp.stack([part] * lax.axis_size(axis)), axis, 0, 0)]
  transfers between devices with their start and end apart: 11 -> 9, of which waited for: 10 -> 8; matrix products, arithmetic and copies ran while one was open for 7% -> 7% of each run, Pallas kernels for 0% -> 0%
where the time goes in v1:
time: 401 us; the launch traced here: 400 us
  waiting for transfers between devices  191 us (48%)
  blocking collectives  105 us (26%)
  local copies, waits for them, and re-layouts  26 us (6%)
  matrix products  24.3 us (6%)
  other arithmetic  21.5 us (5%)
  starting transfers between devices  18.3 us (5%)
  between operations  14.1 us (4%)
    reduce_scatter x2, waiting for transfers between devices, native_scatter(): total = lax.psum_scatter(chunks, axis, scatter_dimension=0, tiled=False)  130 us
    all_to_all x3, blocking collectives, exchange_scatter(): got = lax.all_to_all(chunks, axis, 0, 0, tiled=False)  67.1 us
    all_to_all x2, blocking collectives, native_gather(): lax.all_to_all(jnp.stack([part] * lax.axis_size(axis)), axis, 0, 0)  38.1 us
    all_to_all x3, waiting for transfers between devices, exchange_gather(): lax.all_to_all(jnp.broadcast_to(part[None], (size,) + part.shape), axis,...  27.6 us
    all_gather x1, waiting for transfers between devices, on_device(): gathered = lax.all_gather(summaries, 'landmark', axis=1, tiled=True)  26.2 us
    all_to_all x3, starting transfers between devices, exchange_gather(): lax.all_to_all(jnp.broadcast_to(part[None], (size,) + part.shape), axis,...  10.7 us
    gather x1, local copies, waits for them, and re-layouts, on_device(): anchors = jnp.take(pool, landmark_index, axis=0)  8.79 us
  transfers between devices with their start and end apart: 9, of which 8 were waited for; matrix products, arithmetic and copies ran while one was open for 7% of the time, Pallas kernels for 0%

profile of v1, /device:TPU:0, one launch (start us, length us, event | category | flops | bytes accessed | tf_op | source)
XLA Modules:
  0.0 400.3 jit_solution(875975193546893316)
XLA Ops:
  8.6 5.7 %gather_fusion.1 = s32[1024]{0:T(1024)S(1)} fusion(s32[2048]{0:T(1024)} %param.10, s32[1024]{0:T(1024)S(1)} %fusion.14), kind=kCustom, calls=%fused_computation.1 | custom fusion | bytes 12288 | tf_op jit(solution)/shard_map/jit(_take)/gather | solution.py:199
  14.4 8.8 %gather_fusion = bf16[1024,1024]{1,0:T(8,128)(2,1)} fusion(bf16[2048,1024]{1,0:T(8,128)(2,1)} %param.9, s32[1024]{0:T(1024)S(1)} %fusion.14), kind=kCustom, calls=%fused_computation | custom fusion | bytes 4198400 | tf_op jit(solution)/shard_map/jit(_take)/gather | solution.py:198
  23.4 26.2 %all-gather.2.cloned.1.call-done = bf16[2048,1024]{0,1:T(8,128)(2,1)} async-done(((bf16[2048,64]{0,1:T(8,128)(2,1)}), bf16[2048,1024]{0,1:T(8,128)(2,1)}) %all-gather.2.cloned.1.call-update) | async-done | bytes 4194320 | tf_op jit(solution)/shard_map/all_gather | solution.py:196
  49.6 7.9 %fusion = (f32[1024]{0:T(1024)S(1)}, f32[1024,2048]{1,0:T(8,128)S(1)}) fusion(f32[1024]{0:T(1024)S(1)} %broadcast_divide_fusion.1, f32[2048]{0:T(1024)S(1)} %broadcast_divide_fusion, bf16[2048,1024]{0,1:T(8,128)(2,1)} %all-gather.2.cloned.1.call-done, bf16[1024,1024]{1,0:T(8,128)(2,1)} %gather_fusion, pred[1024]{0:T(1024)(128)(4,1)S(1)} %get-tuple-element.5), kind=kOutput, calls=%fused_computation.4 | convolution fusion | flops 4302306304 | bytes 14697472 | tf_op jit(solution)/shard_map/dot_general | solution.py:26
  75.2 20.1 %all_to_all.40 = f32[8,128,256]{2,1,0:T(8,128)S(1)} all-to-all(f32[8,128,256]{2,1,0:T(8,128)S(1)} %bitcast.107), channel_id=1, replica_groups=mesh['sample'=8,'landmark'=16] {'sample'}, dimensions={0} | all-to-all | bytes 2097152 | tf_op jit(solution)/shard_map/all_to_all | solution.py:104
  96.4 3.6 all-to-all-start.1
  100.2 5.6 %fusion.40 = bf16[2048,1024]{0,1:T(8,128)(2,1)} fusion(f32[1024]{0:T(1024)S(1)} %add_multiply_fusion, f32[1024]{0:T(1024)S(1)} %broadcast_divide_fusion.1, f32[1024,2048]{1,0:T(8,128)} %copy-done.2, f32[2048]{0:T(1024)S(1)} %broadcast_divide_fusion), kind=kLoop, calls=%fused_computation.74 | loop fusion | flops 8388608 | bytes 12599296 | tf_op jit(solution)/shard_map/sub | solution.py:204
  105.9 6.4 %copy.15 = bf16[2048,1024]{1,0:T(8,128)(2,1)} copy(bf16[2048,1024]{0,1:T(8,128)(2,1)} %fusion.40) | data formatting | bytes 8388608 | tf_op jit(solution)/shard_map/dot_general | solution.py:153
  112.5 3.5 fusion.25
  117.6 66.3 %reduce-scatter.3.cloned.1.call-done = f32[1,130,256]{2,1,0:T(8,128)} async-done(((f32[16,130,256]{2,1,0:T(8,128)}), f32[1,130,256]{2,1,0:T(8,128)}) %reduce-scatter.3.cloned.1.call-update) | async-done | bytes 133136 | tf_op jit(solution)/shard_map/reduce_scatter | solution.py:133
  184.9 19.1 %all_to_all.41 = bf16[16,128,256]{2,1,0:T(8,128)(2,1)S(1)} all-to-all(bf16[16,128,256]{2,1,0:T(8,128)(2,1)S(1)} %stack.9), channel_id=1, replica_groups=mesh['sample'=8,'landmark'=16] {'landmark'}, dimensions={0} | all-to-all | bytes 2097152 | tf_op jit(solution)/shard_map/all_to_all | solution.py:139
  203.9 3.4 fusion.26
  207.8 23.6 %all_to_all.42 = f32[8,129,256]{2,1,0:T(8,128)S(1)} all-to-all(f32[8,129,256]{2,1,0:T(8,128)S(1)} %pad_maximum_fusion.2), channel_id=1, replica_groups=mesh['sample'=8,'landmark'=16] {'sample'}, dimensions={0} | all-to-all | bytes 2113536 | tf_op jit(solution)/shard_map/all_to_all | solution.py:104
  232.5 3.6 all-to-all-start.4
  236.2 14.2 %all-to-all-done.4 = f32[8,128,256]{2,1,0:T(8,128)S(1)} async-done(((f32[8,128,256]{2,1,0:T(8,128)}), f32[8,128,256]{2,1,0:T(8,128)S(1)}, u32[]{:S(2)}, u32[]{:S(2)}) %all-to-all-start.4) | async-done | bytes 1048608 | tf_op jit(solution)/shard_map/all_to_all | solution.py:114
  251.7 4.8 %fusion.27 = f32[16,128,256]{2,1,0:T(8,128)} fusion(bf16[16,128,1024]{2,1,0:T(8,128)(2,1)} %bitcast.104, bf16[1024,256,1]{1,0,2:T(8,128)(2,1)S(1)} %bitcast.109), kind=kOutput, calls=%fused_computation.72 | convolution fusion | flops 1073741824 | bytes 6815744 | tf_op jit(solution)/shard_map/dot_general | solution.py:163
  256.5 3.2 pad_maximum_fusion.1
  259.7 63.6 %reduce-scatter.5.cloned.1.call-done = f32[1,130,256]{2,1,0:T(8,128)} async-done(((f32[16,130,256]{2,1,0:T(8,128)}), f32[1,130,256]{2,1,0:T(8,128)}) %reduce-scatter.5.cloned.1.call-update) | async-done | bytes 133136 | tf_op jit(solution)/shard_map/reduce_scatter | solution.py:133
  325.1 19.1 %all_to_all.43 = bf16[16,128,256]{2,1,0:T(8,128)(2,1)S(1)} all-to-all(bf16[16,128,256]{2,1,0:T(8,128)(2,1)S(1)} %stack.11), channel_id=1, replica_groups=mesh['sample'=8,'landmark'=16] {'landmark'}, dimensions={0} | all-to-all | bytes 2097152 | tf_op jit(solution)/shard_map/all_to_all | solution.py:139
  344.1 3.4 fusion.28
  348.0 23.5 %all_to_all.44 = f32[8,129,256]{2,1,0:T(8,128)S(1)} all-to-all(f32[8,129,256]{2,1,0:T(8,128)S(1)} %pad_maximum_fusion.3), channel_id=1, replica_groups=mesh['sample'=8,'landmark'=16] {'sample'}, dimensions={0} | all-to-all | bytes 2113536 | tf_op jit(solution)/shard_map/all_to_all | solution.py:104
  372.6 3.6 all-to-all-start.7
  377.0 13.4 %all-to-all-done.7 = f32[8,128,256]{2,1,0:T(8,128)S(1)} async-done(((f32[8,128,256]{2,1,0:T(8,128)}), f32[8,128,256]{2,1,0:T(8,128)S(1)}, u32[]{:S(2)}, u32[]{:S(2)}) %all-to-all-start.7) | async-done | bytes 1048608 | tf_op jit(solution)/shard_map/all_to_all | solution.py:114
  390.5 3.2 fusion.5
  (73 shorter events, 30.7 us)
Async XLA Ops:
  7.2 66.1 %copy-start = (bf16[2048,256]{1,0:T(8,128)(2,1)S(1)}, bf16[2048,256]{1,0:T(8,128)(2,1)}, u32[]{:S(2)}) copy-start(bf16[2048,256]{1,0:T(8,128)(2,1)} %param.13) | copy-start | bytes 3145732
  7.2 42.4 %all-gather.2.cloned.1.call-start = ((), (), s32[]{:S(2)}) async-start(), calls=%async_computation.10 | async-start | bytes 4456448 | tf_op jit(solution)/shard_map/all_gather | solution.py:196
  14.3 8.8 %copy-start.5 = (s32[1024]{0:T(1024)S(1)}, s32[1024]{0:T(1024)}, u32[]{:S(2)}) copy-start(s32[1024]{0:T(1024)} %param.11) | copy-start | bytes 12292
  14.4 8.8 %copy-start.7 = (f32[4]{0:T(128)S(1)}, f32[4]{0:T(128)}, u32[]{:S(2)}) copy-start(f32[4]{0:T(128)} %param.12) | copy-start | bytes 52
  14.4 8.9 %copy-start.6 = (s32[2048]{0:T(1024)S(1)}, s32[2048]{0:T(1024)}, u32[]{:S(2)}) copy-start(s32[2048]{0:T(1024)} %param.8) | copy-start | bytes 24580
  57.5 15.8 %copy-start.2 = (f32[1024,2048]{1,0:T(8,128)}, f32[1024,2048]{1,0:T(8,128)S(1)}, u32[]{:S(2)}) copy-start(f32[1024,2048]{1,0:T(8,128)S(1)} %get-tuple-element.13) | copy-start | bytes 25165828
  57.5 3.7 collective-permute-start
  61.2 5.1 %collective-permute-start.1 = (f32[1024]{0:T(1024)S(1)}, f32[1024]{0:T(1024)S(1)}, u32[]{:S(2)}, u32[]{:S(2)}) collective-permute-start(f32[1024]{0:T(1024)S(1)} %add.76), channel_id=1, source_target_pairs={{0,16},{16,0},{32,48},{48,32},{64,80},{80,64},{96,112},{112,96},{1... | collective-permute-start | bytes 12296 | tf_op jit(solution)/shard_map/ppermute | solution.py:40
  66.3 5.1 %collective-permute-start.2 = (f32[1024]{0:T(1024)S(1)}, f32[1024]{0:T(1024)S(1)}, u32[]{:S(2)}, u32[]{:S(2)}) collective-permute-start(f32[1024]{0:T(1024)S(1)} %add.77), channel_id=1, source_target_pairs={{0,64},{16,80},{32,96},{48,112},{64,0},{80,16},{96,32},{112,48},{1... | collective-permute-start | bytes 12296 | tf_op jit(solution)/shard_map/ppermute | solution.py:40
  73.3 2.0 copy-start.3
  96.4 15.8 %all-to-all-start.1 = ((f32[8,128,256]{2,1,0:T(8,128)}), f32[8,128,256]{2,1,0:T(8,128)S(1)}, u32[]{:S(2)}, u32[]{:S(2)}) async-start(f32[8,128,256]{2,1,0:T(8,128)} %broadcast_in_dim.115), calls=%async_computation.1 | async-start | bytes 2097152 | tf_op jit(solution)/shard_map/all_to_all | solution.py:114
  100.0 83.9 %reduce-scatter.3.cloned.1.call-start = ((), (), s32[]{:S(2)}) async-start(), calls=%async_computation.11 | async-start | bytes 2367488 | tf_op jit(solution)/shard_map/reduce_scatter | solution.py:133
  207.7 28.4 %copy-start.4 = (f32[1,130,256]{2,1,0:T(8,128)S(1)}, f32[1,130,256]{2,1,0:T(8,128)}, u32[]{:S(2)}) copy-start(f32[1,130,256]{2,1,0:T(8,128)} %reduce-scatter.3.cloned.1.call-done) | copy-start | bytes 399364
  232.5 17.8 %all-to-all-start.4 = ((f32[8,128,256]{2,1,0:T(8,128)}), f32[8,128,256]{2,1,0:T(8,128)S(1)}, u32[]{:S(2)}, u32[]{:S(2)}) async-start(f32[8,128,256]{2,1,0:T(8,128)} %broadcast_in_dim.119), calls=%async_computation.5 | async-start | bytes 2097152 | tf_op jit(solution)/shard_map/all_to_all | solution.py:114
  236.1 87.2 %reduce-scatter.5.cloned.1.call-start = ((), (), s32[]{:S(2)}) async-start(), calls=%async_computation.12 | async-start | bytes 2367488 | tf_op jit(solution)/shard_map/reduce_scatter | solution.py:133
  372.6 17.8 %all-to-all-start.7 = ((f32[8,128,256]{2,1,0:T(8,128)}), f32[8,128,256]{2,1,0:T(8,128)S(1)}, u32[]{:S(2)}, u32[]{:S(2)}) async-start(f32[8,128,256]{2,1,0:T(8,128)} %broadcast_in_dim.123), calls=%async_computation.9 | async-start | bytes 2097152 | tf_op jit(solution)/shard_map/all_to_all | solution.py:114
  376.2 17.6 %copy-start.1 = (bf16[2048,256]{1,0:T(8,128)(2,1)S(1)}, bf16[2048,256]{1,0:T(8,128)(2,1)}, u32[]{:S(2)}) copy-start(bf16[2048,256]{1,0:T(8,128)(2,1)} %param.13) | copy-start | bytes 3145732
Sparse Core Ops, SparseCore 0:
  9.7 39.8 all-gather.1
  117.7 66.1 reduce-scatter.2
  259.9 63.4 reduce-scatter.4
